TPU v7x, 512 devices: a whole 4x8x8 slice. The times are simulated.
512 devices in a mesh: pb: 32 (over y, x), ka: 16 (over z, core).
Axes of the slice: x: 4, y: 8, z: 8, core: 2. Of those that a mesh axis runs over, the one named last changes fastest.
Arguments:
- queries: bfloat16 [65536, 1536], P(('pb', 'ka')), may hold values from -6 to 6
- keys: bfloat16 [65536, 1536], P(('pb', 'ka')), may hold values from -6 to 6
- values: bfloat16 [65536, 1536], P(('pb', 'ka')), may hold values from -6 to 6
- adjacency: int32 [512, 24], P(('pb', 'ka')), may hold values from -1 to 511, as said below
- counts: int32 [512], P(('pb', 'ka')), may hold values from 1 to 24, as said below
Outputs:
- attended: bfloat16 [65536, 1536], P(('pb', 'ka'))
Inputs may be any that keep to these rules, and one draw needn't show every extreme that they name: adjacency[i, 0] = i; entries 1 to counts[i] - 1 are distinct blocks from i - 31 to i - 1; the other entries are -1. counts[i] is at most min(i + 1, 32); the last block lists exactly 24.
All inputs are finite; a program needn't handle non-finite values.
Results may differ from a plain program's by a relative error of at most 0.0053.
Values may be sent and summed in bfloat16 or wider, within the bound.
No kernel may reach another device: no remote copies, remote signals or barrier semaphores. Data moves between devices by JAX's collectives and lax.ppermute only.
A program may use at most 128 MiB of HBM per device.

v0:
```python
import math
import jax
import jax.numpy as jnp
from jax import lax
from jax.sharding import PartitionSpec as P

DH = 128
NEG_FILL = -1e30


def passed_along(block, axis, distance):
    devices = range(lax.axis_size(axis))
    route = [(i - distance, i) for i in devices if i - distance in devices]
    return lax.ppermute(block, axis, route)


def tile_partials(query_rows, permitted, position, anchors, kv_window, current):
    sources, item_count, feature_width = query_rows.shape
    span_count = kv_window.shape[1]
    block_len = kv_window.shape[2]
    head_count = feature_width // DH
    grouped = math.gcd(sources, max(1, 512 // item_count))
    head_step = math.gcd(head_count, 4)
    scaling = 1.0 / math.sqrt(DH)
    key_window = kv_window[0].reshape(span_count, block_len, head_count, DH)
    value_window = kv_window[1].reshape(span_count, block_len, head_count, DH)
    leading = jnp.arange(span_count) == 0
    key_pos = jnp.arange(block_len, dtype=jnp.int32)

    def one_group(pieces):
        q_group, allow_group, pos_group, anchor_group = pieces
        q_group = q_group.reshape(grouped, item_count, head_count, DH)
        causal = key_pos[None, None, None, :] <= pos_group[:, :, None, None]
        own_block = (anchor_group == current)[:, None] & leading[None, :]
        allowed = (allow_group[:, :, :, None] != 0) & (
            jnp.logical_not(own_block)[:, None, :, None] | causal
        )
        part_list = []
        max_list = []
        total_list = []
        for head_lo in range(0, head_count, head_step):
            head_hi = head_lo + head_step
            scores = (
                jnp.einsum(
                    "gthd,auhd->ghtau",
                    q_group[:, :, head_lo:head_hi],
                    key_window[:, :, head_lo:head_hi],
                    preferred_element_type=jnp.float32,
                )
                * scaling
            )
            masked = jnp.where(allowed[:, None], scores, NEG_FILL)
            highest = jnp.max(masked, axis=(3, 4))
            weights = jnp.where(allowed[:, None], jnp.exp(masked - highest[..., None, None]), 0.0)
            total_list.append(jnp.sum(weights, axis=(3, 4)))
            max_list.append(highest)
            blended = jnp.einsum(
                "ghtau,auhd->gthd",
                weights.astype(jnp.bfloat16),
                value_window[:, :, head_lo:head_hi],
                preferred_element_type=jnp.float32,
            )
            part_list.append(blended.astype(jnp.bfloat16))
        partial_out = jnp.concatenate(part_list, axis=2).reshape(grouped, item_count, feature_width)
        class_max = jnp.transpose(jnp.concatenate(max_list, axis=1), (0, 2, 1))
        class_total = jnp.transpose(jnp.concatenate(total_list, axis=1), (0, 2, 1))
        return (partial_out, class_max, class_total)

    outer = sources // grouped
    reshaped = (
        query_rows.reshape(outer, grouped, item_count, feature_width),
        permitted.reshape(outer, grouped, item_count, span_count),
        position.reshape(outer, grouped, item_count),
        anchors.reshape(outer, grouped),
    )
    partial_out, class_max, class_total = lax.map(one_group, reshaped)
    return (
        partial_out.reshape(sources, item_count, feature_width).astype(jnp.float32),
        class_max.reshape(sources, item_count, head_count),
        class_total.reshape(sources, item_count, head_count),
    )


def merge_classes(partial_out, class_max, class_total):
    sources, block_len, feature_width = partial_out.shape
    head_count = class_max.shape[2]
    highest = jnp.max(class_max, axis=0)
    factor = jnp.exp(class_max - highest[None])
    denominator = jnp.sum(factor * class_total, axis=0)
    numerator = jnp.sum(
        factor[..., None] * partial_out.reshape(sources, block_len, head_count, DH), axis=0
    )
    return (
        (numerator / denominator[..., None]).reshape(block_len, feature_width).astype(jnp.bfloat16)
    )


def per_device(queries, keys, values, adjacency, counts):
    block_len, feature_width = queries.shape
    stripe_count = lax.axis_size("ka")
    current = lax.axis_index("ka")
    row_index = lax.axis_index("pb")
    stacked = jnp.stack([keys, values])
    window = [stacked]
    earlier = stacked
    for repeat in range(2):
        earlier = passed_along(earlier, "pb", 1)
        window.append(earlier)
    kv_window = jnp.stack(window, axis=1)
    span_count = len(window)
    lag_ids = jnp.arange(span_count, dtype=jnp.int32)
    slot_ids = jnp.arange(adjacency.shape[1], dtype=jnp.int32)
    positions = jnp.broadcast_to(
        jnp.arange(block_len, dtype=jnp.int32)[None, :], (stripe_count, block_len)
    )
    anchors = jnp.arange(stripe_count, dtype=jnp.int32)
    row_q, row_adj, row_cnt = (
        lax.all_gather(queries, "ka", axis=0, tiled=True),
        lax.all_gather(adjacency, "ka", axis=0, tiled=True),
        lax.all_gather(counts, "ka", axis=0, tiled=True),
    )
    wanted = (row_index - lag_ids) * stripe_count + current
    listed = (row_adj[:, None, :] == wanted[None, :, None]) & (
        slot_ids[None, None, :] < row_cnt[:, None, None]
    )
    present = jnp.any(listed, axis=2).astype(jnp.int32)
    permitted = jnp.broadcast_to(present[:, None, :], (stripe_count, block_len, span_count))
    partial_out, class_max, class_total = tile_partials(
        row_q.reshape(stripe_count, block_len, feature_width),
        permitted,
        positions,
        anchors,
        kv_window,
        current,
    )
    partial_out, class_max, class_total = (
        lax.all_to_all(partial_out, "ka", split_axis=0, concat_axis=0, tiled=True),
        lax.all_to_all(class_max, "ka", split_axis=0, concat_axis=0, tiled=True),
        lax.all_to_all(class_total, "ka", split_axis=0, concat_axis=0, tiled=True),
    )
    return merge_classes(partial_out, class_max, class_total)


def solution(mesh):
    in_specs = (
        P(("pb", "ka"), None),
        P(("pb", "ka"), None),
        P(("pb", "ka"), None),
        P(("pb", "ka"), None),
        P(("pb", "ka")),
    )
    out_specs = P(("pb", "ka"), None)
    return jax.shard_map(
        per_device, mesh=mesh, in_specs=in_specs, out_specs=out_specs, check_vma=False
    )
```

profile of v0, /device:TPU:30, one launch (start us, length us, event | category | flops | bytes accessed | tf_op | source)
XLA Modules:
  0.0 505.4 jit_solution(13718441947726245500)
XLA Ops:
  7.3 1.2 copy.75
  8.5 1.2 copy.76
  9.8 4.6 collective-permute-start
  14.4 16.8 %collective-permute-done = bf16[2,128,1536]{1,2,0:T(8,128)(2,1)S(1)} collective-permute-done((bf16[2,128,1536]{1,2,0:T(8,128)(2,1)S(1)}, bf16[2,128,1536]{1,2,0:T(8,128)(2,1)S(1)}, u32[]{:S(2)}, u32[]{:S(2)}) %collective-permute-start) | collective-permute-done | bytes 786464 | tf_op jit(solution)/shard_map/ppermute | solution.py:14
  31.2 7.7 %collective-permute-start.1 = (bf16[2,128,1536]{1,2,0:T(8,128)(2,1)S(1)}, bf16[2,128,1536]{1,2,0:T(8,128)(2,1)S(1)}, u32[]{:S(2)}, u32[]{:S(2)}) collective-permute-start(bf16[2,128,1536]{1,2,0:T(8,128)(2,1)S(1)} %collective-permute-done), channel_id=1, source_target_pairs={{0,16},{16,32},{32,48},{48,64},{64,80},{80,96},{96,112},{112,128},... | collective-permute-start | bytes 2359304 | tf_op jit(solution)/shard_map/ppermute | solution.py:14
  39.6 1.3 dynamic-slice
  41.5 20.1 %all-reduce = s32[16]{0:T(128)S(1)} all-reduce(s32[16]{0:T(128)S(1)} %dynamic-update-slice), channel_id=1, replica_groups=mesh['pb'=32,'ka'=16] {'ka'}, use_global_device_ids=true, to_apply=%add | all-reduce | flops 16 | bytes 128
  61.6 15.1 %all-gather = s32[16,1,24]{2,1,0:T(1,128)S(1)} all-gather(s32[1,1,24]{2,1,0:T(1,128)S(1)} %bitcast.255), channel_id=1, replica_groups=mesh['pb'=32,'ka'=16] {'ka'}, dimensions={0}, use_global_device_ids=true | all-gather | bytes 1632 | tf_op jit(solution)/shard_map/all_gather | solution.py:119
  77.6 1.4 copy.80
  79.0 1.1 copy.81
  80.2 105.2 %while.15 = (s32[]{:T(128)}, bf16[4,4,128,1536]{2,3,1,0:T(8,128)(2,1)}, f32[4,4,128,12]{2,1,0,3:T(4,128)S(1)}, f32[4,4,128,12]{2,1,0,3:T(4,128)}, s32[4,4,128,3]...) while((s32[]{:T(128)}, ...), condition=%wide.region_8.9_spmd.clone, body=%wide.region_1.8_spmd.clone.sunk | while | flops 1241462272 | bytes 78790904 | solution.py:76
  80.6 1.5 constant_dynamic-slice_fusion.3
  83.0 1.1 fusion.116
  84.1 1.0 copy.119
  85.2 1.7 fusion.117
  86.9 2.0 copy.120
  88.9 4.0 bitcast_reduce_fusion.4
  92.9 2.0 copy.121
  95.0 4.6 fusion.118
  101.5 1.1 fusion.121
  102.6 1.1 fusion.120
  103.7 1.1 fusion.119
  105.2 1.3 constant_dynamic-update-slice_fusion.2
  106.9 1.5 constant_dynamic-slice_fusion.3
  109.3 1.1 fusion.116
  111.5 1.7 fusion.117
  113.2 2.0 copy.120
  115.2 4.0 bitcast_reduce_fusion.4
  119.2 2.0 copy.121
  121.3 4.6 fusion.118
  127.8 1.1 fusion.121
  128.9 1.1 fusion.120
  130.0 1.1 fusion.119
  131.5 1.3 constant_dynamic-update-slice_fusion.2
  133.1 1.5 constant_dynamic-slice_fusion.3
  135.6 1.1 fusion.116
  137.7 1.7 fusion.117
  139.5 2.0 copy.120
  141.5 4.0 bitcast_reduce_fusion.4
  145.5 2.0 copy.121
  147.5 4.6 fusion.118
  154.1 1.1 fusion.121
  155.2 1.1 fusion.120
  156.3 1.1 fusion.119
  157.8 1.3 constant_dynamic-update-slice_fusion.2
  159.4 1.5 constant_dynamic-slice_fusion.3
  161.8 1.1 fusion.116
  164.0 1.7 fusion.117
  165.7 2.0 copy.120
  167.8 4.0 bitcast_reduce_fusion.4
  171.8 2.0 copy.121
  173.8 4.7 fusion.118
  180.4 1.1 fusion.121
  181.5 1.1 fusion.120
  182.6 1.1 fusion.119
  184.1 1.3 constant_dynamic-update-slice_fusion.2
  186.0 3.9 all-to-all-start
  190.0 1.6 copy.85
  191.6 7.1 %all-to-all-done = f32[16,128,12]{1,2,0:T(8,128)S(1)} async-done(((f32[16,128,12]{1,2,0:T(8,128)}), f32[16,128,12]{1,2,0:T(8,128)S(1)}, u32[]{:S(2)}, u32[]{:S(2)}) %all-to-all-start) | async-done | bytes 98336 | tf_op jit(solution)/shard_map/all_to_all | solution.py:138
  198.6 3.7 all-to-all-start.2
  202.3 8.6 %bitcast_convert_fusion = f32[16,128,1536]{1,2,0:T(8,128)} fusion(bf16[4,4,128,1536]{2,3,1,0:T(8,128)(2,1)} %get-tuple-element.75), kind=kLoop, calls=%fused_computation.86 | loop fusion | flops 3145728 | bytes 18874368 | tf_op jit(solution)/shard_map/convert_element_type | solution.py:78
  211.0 7.0 %all-to-all-start.1 = ((f32[16,128,1536]{1,2,0:T(8,128)}), f32[16,128,1536]{1,2,0:T(8,128)}, u32[]{:S(2)}, u32[]{:S(2)}) async-start(f32[16,128,1536]{1,2,0:T(8,128)} %bitcast_convert_fusion), calls=%async_computation.1 | async-start | bytes 25165824 | tf_op jit(solution)/shard_map/all_to_all | solution.py:137
  218.0 274.0 %all-to-all-done.1 = f32[16,128,1536]{1,2,0:T(8,128)} async-done(((f32[16,128,1536]{1,2,0:T(8,128)}), f32[16,128,1536]{1,2,0:T(8,128)}, u32[]{:S(2)}, u32[]{:S(2)}) %all-to-all-start.1) | async-done | bytes 12582944 | tf_op jit(solution)/shard_map/all_to_all | solution.py:137
  492.0 5.6 %fusion.85 = f32[128,1536]{0,1:T(8,128)S(1)} fusion(f32[16,128,1536]{1,2,0:T(8,128)} %all-to-all-done.1, f32[16,128,12]{1,2,0:T(8,128)S(1)} %get-tuple-element.174), kind=kLoop, calls=%fused_computation.85 | loop fusion | flops 6094848 | bytes 13467648 | tf_op jit(solution)/shard_map/reduce_sum | solution.py:90
  (95 shorter events, 21.1 us)
Async XLA Ops:
  6.5 55.1 %copy-start.2 = (s32[1,24]{1,0:T(1,128)S(1)}, s32[1,24]{1,0:T(1,128)}, u32[]{:S(2)}) copy-start(s32[1,24]{1,0:T(1,128)} %param.10) | copy-start | bytes 292
  6.5 73.6 %all-gather.3.cloned.1.call-start = ((), (), s32[]{:S(2)}) async-start(), calls=%async_computation.3 | async-start | bytes 6684672 | tf_op jit(solution)/shard_map/all_gather | solution.py:118
  9.8 21.4 %collective-permute-start = (bf16[2,128,1536]{1,2,0:T(8,128)(2,1)S(1)}, bf16[2,128,1536]{1,2,0:T(8,128)(2,1)S(1)}, u32[]{:S(2)}, u32[]{:S(2)}) collective-permute-start(bf16[2,128,1536]{1,2,0:T(8,128)(2,1)S(1)} %get-tuple-element.185), channel_id=1, source_target_pairs={{0,16},{16,32},{32,48},{48,64},{64,80},{80,96},{96,112},{112,128},... | collective-permute-start | bytes 2359304 | tf_op jit(solution)/shard_map/ppermute | solution.py:14
  31.2 46.0 %collective-permute-start.1 = (bf16[2,128,1536]{1,2,0:T(8,128)(2,1)S(1)}, bf16[2,128,1536]{1,2,0:T(8,128)(2,1)S(1)}, u32[]{:S(2)}, u32[]{:S(2)}) collective-permute-start(bf16[2,128,1536]{1,2,0:T(8,128)(2,1)S(1)} %collective-permute-done), channel_id=1, source_target_pairs={{0,16},{16,32},{32,48},{48,64},{64,80},{80,96},{96,112},{112,128},... | collective-permute-start | bytes 2359304 | tf_op jit(solution)/shard_map/ppermute | solution.py:14
  95.0 6.1 %copy-start.1 = (bf16[3,128,12,128]{1,3,0,2:T(8,128)(2,1)S(1)}, bf16[3,128,12,128]{1,3,0,2:T(8,128)(2,1)}, u32[]{:S(2)}) copy-start(bf16[3,128,12,128]{1,3,0,2:T(8,128)(2,1)} %get-tuple-element.311) | copy-start | bytes 3538948 | tf_op jit(solution)/shard_map/while
  99.6 1.9 copy-start
  121.3 6.1 %copy-start.1 = (bf16[3,128,12,128]{1,3,0,2:T(8,128)(2,1)S(1)}, bf16[3,128,12,128]{1,3,0,2:T(8,128)(2,1)}, u32[]{:S(2)}) copy-start(bf16[3,128,12,128]{1,3,0,2:T(8,128)(2,1)} %get-tuple-element.311) | copy-start | bytes 3538948 | tf_op jit(solution)/shard_map/while
  125.9 1.9 copy-start
  147.5 6.1 %copy-start.1 = (bf16[3,128,12,128]{1,3,0,2:T(8,128)(2,1)S(1)}, bf16[3,128,12,128]{1,3,0,2:T(8,128)(2,1)}, u32[]{:S(2)}) copy-start(bf16[3,128,12,128]{1,3,0,2:T(8,128)(2,1)} %get-tuple-element.311) | copy-start | bytes 3538948 | tf_op jit(solution)/shard_map/while
  152.2 1.9 copy-start
  173.8 6.1 %copy-start.1 = (bf16[3,128,12,128]{1,3,0,2:T(8,128)(2,1)S(1)}, bf16[3,128,12,128]{1,3,0,2:T(8,128)(2,1)}, u32[]{:S(2)}) copy-start(bf16[3,128,12,128]{1,3,0,2:T(8,128)(2,1)} %get-tuple-element.311) | copy-start | bytes 3538948 | tf_op jit(solution)/shard_map/while
  178.5 1.9 copy-start
  186.0 12.6 %all-to-all-start = ((f32[16,128,12]{1,2,0:T(8,128)}), f32[16,128,12]{1,2,0:T(8,128)S(1)}, u32[]{:S(2)}, u32[]{:S(2)}) async-start(f32[16,128,12]{1,2,0:T(8,128)} %copy.83), calls=%async_computation | async-start | bytes 262144 | tf_op jit(solution)/shard_map/all_to_all | solution.py:138
  198.6 12.3 %all-to-all-start.2 = ((f32[16,128,12]{1,2,0:T(8,128)}), f32[16,128,12]{1,2,0:T(8,128)S(1)}, u32[]{:S(2)}, u32[]{:S(2)}) async-start(f32[16,128,12]{1,2,0:T(8,128)} %copy.85), calls=%async_computation.2 | async-start | bytes 262144 | tf_op jit(solution)/shard_map/all_to_all | solution.py:139
  211.0 281.0 %all-to-all-start.1 = ((f32[16,128,1536]{1,2,0:T(8,128)}), f32[16,128,1536]{1,2,0:T(8,128)}, u32[]{:S(2)}, u32[]{:S(2)}) async-start(f32[16,128,1536]{1,2,0:T(8,128)} %bitcast_convert_fusion), calls=%async_computation.1 | async-start | bytes 25165824 | tf_op jit(solution)/shard_map/all_to_all | solution.py:137
Sparse Core Ops, SparseCore 0:
  9.5 53.8 all-gather.2
where the time goes:
time: 507 us; the launch traced here: 505 us
  waiting for transfers between devices  299 us (59%)
  matrix products  54.7 us (11%)
  local copies, waits for them, and re-layouts  52.6 us (10%)
  blocking collectives  35.2 us (7%)
  starting transfers between devices  26.9 us (5%)
  other arithmetic  22.8 us (4%)
  between operations  14.2 us (3%)
    all_to_all x1, waiting for transfers between devices, per_device(): lax.all_to_all(partial_out, 'ka', split_axis=0, concat_axis=0, tiled=True)  274 us
    dot_general x12, matrix products, one_group(): jnp.einsum('gthd,auhd->ghtau', q_group[:, :, head_lo:head_hi], key_window...  41.4 us
    while x28, local copies, waits for them, and re-layouts  22.3 us
    unnamed x1, blocking collectives  20.1 us
    ppermute x2, waiting for transfers between devices, passed_along(): return lax.ppermute(block, axis, route)  16.8 us
    all_gather x1, blocking collectives, per_device(): lax.all_gather(adjacency, 'ka', axis=0, tiled=True)  15.1 us
    dot_general x12, matrix products, one_group(): jnp.einsum('ghtau,auhd->gthd', weights.astype(jnp.bfloat16), value_window...  13.3 us
    ppermute x2, starting transfers between devices, passed_along(): return lax.ppermute(block, axis, route)  12.3 us
  transfers between devices with their start and end apart: 6, of which 3 were waited for; matrix products, arithmetic and copies ran while one was open for 4% of the time, Pallas kernels for 0%

commit v1 on v0

--- a/solution.py
+++ b/solution.py
@@ -6,6 +6,19 @@
 
 DH = 128
 NEG_FILL = -1e30
+
+
+def collect(x, axis, dim):
+    ways = lax.axis_size(axis)
+    up = [(d, (d + 1) % ways) for d in range(ways)]
+    down = [(d, (d - 1) % ways) for d in range(ways)]
+    earlier, later = ([x], [x])
+    for _ in range(ways // 2):
+        earlier.append(lax.ppermute(earlier[-1], axis, up))
+    for _ in range((ways - 1) // 2):
+        later.append(lax.ppermute(later[-1], axis, down))
+    line = jnp.concatenate([*earlier[::-1], *later[1:]], axis=dim)
+    return jnp.roll(line, (lax.axis_index(axis) - ways // 2) * x.shape[dim], axis=dim)
 
 
 def passed_along(block, axis, distance):
@@ -116,7 +129,7 @@
     anchors = jnp.arange(stripe_count, dtype=jnp.int32)
     row_q, row_adj, row_cnt = (
         lax.all_gather(queries, "ka", axis=0, tiled=True),
-        lax.all_gather(adjacency, "ka", axis=0, tiled=True),
+        collect(adjacency, "ka", 0),
         lax.all_gather(counts, "ka", axis=0, tiled=True),
     )
     wanted = (row_index - lag_ids) * stripe_count + current

time: 507 us -> 523 us (1.032)
  starting transfers between devices: 26.9 us -> 51.4 us
  blocking collectives: 35.2 us -> 14.5 us
  waiting for transfers between devices: 299 us -> 310 us
    ppermute x0 -> x15, starting transfers between devices: none -> 24.9 us  [the longest x7 24.8 us: collect(): later.append(lax.ppermute(later[-1], axis, down))]
    all_gather x1 -> x0, blocking collectives: 15.1 us -> none  [per_device(): lax.all_gather(adjacency, 'ka', axis=0, tiled=True)]
    ppermute x0 -> x15, waiting for transfers between devices: none -> 11.9 us  [the longest x8 11.6 us: collect(): earlier.append(lax.ppermute(earlier[-1], axis, up))]
    unnamed x1, blocking collectives: 20.1 us -> 14.5 us
  transfers between devices with their start and end apart: 6 -> 21, of which waited for: 3 -> 10; matrix products, arithmetic and copies ran while one was open for 4% -> 3% of each run, Pallas kernels for 0% -> 0%
where the time goes in v1:
time: 523 us; the launch traced here: 521 us
  waiting for transfers between devices  310 us (59%)
  matrix products  54.7 us (10%)
  local copies, waits for them, and re-layouts  52.8 us (10%)
  starting transfers between devices  51.4 us (10%)
  other arithmetic  22.7 us (4%)
  blocking collectives  14.5 us (3%)
  between operations  14.2 us (3%)
    all_to_all x1, waiting for transfers between devices, per_device(): lax.all_to_all(partial_out, 'ka', split_axis=0, concat_axis=0, tiled=True)  274 us
    dot_general x12, matrix products, one_group(): jnp.einsum('gthd,auhd->ghtau', q_group[:, :, head_lo:head_hi], key_window...  41.4 us
    ppermute x7, starting transfers between devices, collect(): later.append(lax.ppermute(later[-1], axis, down))  24.8 us
    while x28, local copies, waits for them, and re-layouts  22.3 us
    ppermute x2, waiting for transfers between devices, passed_along(): return lax.ppermute(block, axis, route)  16.8 us
    unnamed x1, blocking collectives  14.5 us
    dot_general x12, matrix products, one_group(): jnp.einsum('ghtau,auhd->gthd', weights.astype(jnp.bfloat16), value_window...  13.3 us
    ppermute x2, starting transfers between devices, passed_along(): return lax.ppermute(block, axis, route)  12.3 us
  transfers between devices with their start and end apart: 21, of which 10 were waited for; matrix products, arithmetic and copies ran while one was open for 3% of the time, Pallas kernels for 0%

profile of v1, /device:TPU:30, one launch (start us, length us, event | category | flops | bytes accessed | tf_op | source)
XLA Modules:
  0.0 521.1 jit_solution(479312939483987374)
XLA Ops:
  7.3 1.2 copy.75
  8.5 1.2 copy.76
  9.8 4.6 collective-permute-start.15
  14.4 16.8 %collective-permute-done.15 = bf16[2,128,1536]{1,2,0:T(8,128)(2,1)S(1)} collective-permute-done((bf16[2,128,1536]{1,2,0:T(8,128)(2,1)S(1)}, bf16[2,128,1536]{1,2,0:T(8,128)(2,1)S(1)}, u32[]{:S(2)}, u32[]{:S(2)}) %collective-permute-start.15) | collective-permute-done | bytes 786464 | tf_op jit(solution)/shard_map/ppermute | solution.py:27
  31.2 7.7 %collective-permute-start.16 = (bf16[2,128,1536]{1,2,0:T(8,128)(2,1)S(1)}, bf16[2,128,1536]{1,2,0:T(8,128)(2,1)S(1)}, u32[]{:S(2)}, u32[]{:S(2)}) collective-permute-start(bf16[2,128,1536]{1,2,0:T(8,128)(2,1)S(1)} %collective-permute-done.15), channel_id=1, source_target_pairs={{0,16},{16,32},{32,48},{48,64},{64,80},{80,96},{96,112},{112,128},... | collective-permute-start | bytes 2359304 | tf_op jit(solution)/shard_map/ppermute | solution.py:27
  39.0 7.4 %collective-permute-start.8 = (s32[1,24]{1,0:T(1,128)S(1)}, s32[1,24]{1,0:T(1,128)S(1)}, u32[]{:S(2)}, u32[]{:S(2)}) collective-permute-start(s32[1,24]{1,0:T(1,128)S(1)} %copy-done.2), channel_id=1, source_target_pairs={{0,15},{1,0},{2,1},{3,2},{4,3},{5,4},{6,5},{7,6},{8,7},{9,8},{10,9... | collective-permute-start | bytes 296 | tf_op jit(solution)/shard_map/ppermute | solution.py:19
  47.0 1.3 dynamic-slice
  48.9 14.5 %all-reduce = s32[16]{0:T(128)S(1)} all-reduce(s32[16]{0:T(128)S(1)} %dynamic-update-slice), channel_id=1, replica_groups=mesh['pb'=32,'ka'=16] {'ka'}, use_global_device_ids=true, to_apply=%add | all-reduce | flops 16 | bytes 128
  63.5 2.9 collective-permute-start.9
  66.4 1.2 collective-permute-done.1
  67.7 2.9 collective-permute-start.10
  70.6 1.2 collective-permute-done.2
  71.9 2.9 collective-permute-start.11
  74.8 1.2 collective-permute-done.3
  76.1 2.9 collective-permute-start.12
  79.1 1.2 collective-permute-done.4
  80.3 2.9 collective-permute-start.13
  83.3 1.2 collective-permute-done.5
  84.6 2.9 collective-permute-start.14
  87.5 1.2 collective-permute-done.6
  88.8 4.2 collective-permute-done.7
  93.8 1.4 copy.80
  96.4 105.1 %while.15 = (s32[]{:T(128)}, bf16[4,4,128,1536]{2,3,1,0:T(8,128)(2,1)}, f32[4,4,128,12]{2,1,0,3:T(4,128)S(1)}, f32[4,4,128,12]{2,1,0,3:T(4,128)}, s32[4,4,128,3]...) while((s32[]{:T(128)}, ...), condition=%wide.region_8.9_spmd.clone, body=%wide.region_1.8_spmd.clone.sunk | while | flops 1241462272 | bytes 78790904 | solution.py:89
  96.8 1.5 constant_dynamic-slice_fusion.4
  99.2 1.1 fusion.116
  101.3 1.7 fusion.117
  103.1 2.0 copy.120
  105.1 4.0 bitcast_reduce_fusion.4
  109.1 2.0 copy.121
  111.1 4.6 fusion.118
  119.9 1.1 fusion.119
  121.4 1.3 constant_dynamic-update-slice_fusion.2
  123.1 1.5 constant_dynamic-slice_fusion.4
  125.5 1.1 fusion.116
  127.6 1.7 fusion.117
  129.4 2.0 copy.120
  131.4 4.0 bitcast_reduce_fusion.4
  135.4 2.0 copy.121
  137.5 4.6 fusion.118
  147.7 1.3 constant_dynamic-update-slice_fusion.2
  149.3 1.5 constant_dynamic-slice_fusion.4
  151.8 1.1 fusion.116
  153.9 1.7 fusion.117
  155.6 2.0 copy.120
  157.7 4.0 bitcast_reduce_fusion.4
  161.7 2.0 copy.121
  163.7 4.6 fusion.118
  174.0 1.3 constant_dynamic-update-slice_fusion.2
  175.6 1.5 constant_dynamic-slice_fusion.4
  178.0 1.1 fusion.116
  180.2 1.7 fusion.117
  181.9 2.0 copy.120
  183.9 4.0 bitcast_reduce_fusion.4
  187.9 2.0 copy.121
  190.0 4.6 fusion.118
  200.2 1.3 constant_dynamic-update-slice_fusion.2
  202.2 3.5 all-to-all-start
  205.7 1.6 copy.85
  207.3 7.0 %all-to-all-done = f32[16,128,12]{1,2,0:T(8,128)S(1)} async-done(((f32[16,128,12]{1,2,0:T(8,128)}), f32[16,128,12]{1,2,0:T(8,128)S(1)}, u32[]{:S(2)}, u32[]{:S(2)}) %all-to-all-start) | async-done | bytes 98336 | tf_op jit(solution)/shard_map/all_to_all | solution.py:151
  214.3 3.7 all-to-all-start.2
  218.0 8.6 %bitcast_convert_fusion = f32[16,128,1536]{1,2,0:T(8,128)} fusion(bf16[4,4,128,1536]{2,3,1,0:T(8,128)(2,1)} %get-tuple-element.75), kind=kLoop, calls=%fused_computation.86 | loop fusion | flops 3145728 | bytes 18874368 | tf_op jit(solution)/shard_map/convert_element_type | solution.py:91
  226.6 7.0 %all-to-all-start.1 = ((f32[16,128,1536]{1,2,0:T(8,128)}), f32[16,128,1536]{1,2,0:T(8,128)}, u32[]{:S(2)}, u32[]{:S(2)}) async-start(f32[16,128,1536]{1,2,0:T(8,128)} %bitcast_convert_fusion), calls=%async_computation.1 | async-start | bytes 25165824 | tf_op jit(solution)/shard_map/all_to_all | solution.py:150
  233.7 274.0 %all-to-all-done.1 = f32[16,128,1536]{1,2,0:T(8,128)} async-done(((f32[16,128,1536]{1,2,0:T(8,128)}), f32[16,128,1536]{1,2,0:T(8,128)}, u32[]{:S(2)}, u32[]{:S(2)}) %all-to-all-start.1) | async-done | bytes 12582944 | tf_op jit(solution)/shard_map/all_to_all | solution.py:150
  507.7 5.6 %fusion.85 = f32[128,1536]{0,1:T(8,128)S(1)} fusion(f32[16,128,1536]{1,2,0:T(8,128)} %all-to-all-done.1, f32[16,128,12]{1,2,0:T(8,128)S(1)} %get-tuple-element.174), kind=kLoop, calls=%fused_computation.85 | loop fusion | flops 6094848 | bytes 13467648 | tf_op jit(solution)/shard_map/reduce_sum | solution.py:103
  (126 shorter events, 35.8 us)
Async XLA Ops:
  6.5 32.4 %copy-start.2 = (s32[1,24]{1,0:T(1,128)S(1)}, s32[1,24]{1,0:T(1,128)}, u32[]{:S(2)}) copy-start(s32[1,24]{1,0:T(1,128)} %param.10) | copy-start | bytes 292
  6.5 89.8 %all-gather.2.cloned.1.call-start = ((), (), s32[]{:S(2)}) async-start(), calls=%async_computation.3 | async-start | bytes 6684672 | tf_op jit(solution)/shard_map/all_gather | solution.py:131
  9.8 21.4 %collective-permute-start.15 = (bf16[2,128,1536]{1,2,0:T(8,128)(2,1)S(1)}, bf16[2,128,1536]{1,2,0:T(8,128)(2,1)S(1)}, u32[]{:S(2)}, u32[]{:S(2)}) collective-permute-start(bf16[2,128,1536]{1,2,0:T(8,128)(2,1)S(1)} %get-tuple-element.185), channel_id=1, source_target_pairs={{0,16},{16,32},{32,48},{48,64},{64,80},{80,96},{96,112},{112,128},... | collective-permute-start | bytes 2359304 | tf_op jit(solution)/shard_map/ppermute | solution.py:27
  31.2 62.1 %collective-permute-start.16 = (bf16[2,128,1536]{1,2,0:T(8,128)(2,1)S(1)}, bf16[2,128,1536]{1,2,0:T(8,128)(2,1)S(1)}, u32[]{:S(2)}, u32[]{:S(2)}) collective-permute-start(bf16[2,128,1536]{1,2,0:T(8,128)(2,1)S(1)} %collective-permute-done.15), channel_id=1, source_target_pairs={{0,16},{16,32},{32,48},{48,64},{64,80},{80,96},{96,112},{112,128},... | collective-permute-start | bytes 2359304 | tf_op jit(solution)/shard_map/ppermute | solution.py:27
  38.9 24.5 %collective-permute-start = (s32[1,24]{1,0:T(1,128)S(1)}, s32[1,24]{1,0:T(1,128)S(1)}, u32[]{:S(2)}, u32[]{:S(2)}) collective-permute-start(s32[1,24]{1,0:T(1,128)S(1)} %copy-done.2), channel_id=1, source_target_pairs={{0,1},{1,2},{2,3},{3,4},{4,5},{5,6},{6,7},{7,8},{8,9},{9,10},{10,1... | collective-permute-start | bytes 296 | tf_op jit(solution)/shard_map/ppermute | solution.py:17
  39.0 24.5 %collective-permute-start.8 = (s32[1,24]{1,0:T(1,128)S(1)}, s32[1,24]{1,0:T(1,128)S(1)}, u32[]{:S(2)}, u32[]{:S(2)}) collective-permute-start(s32[1,24]{1,0:T(1,128)S(1)} %copy-done.2), channel_id=1, source_target_pairs={{0,15},{1,0},{2,1},{3,2},{4,3},{5,4},{6,5},{7,6},{8,7},{9,8},{10,9... | collective-permute-start | bytes 296 | tf_op jit(solution)/shard_map/ppermute | solution.py:19
  63.5 4.2 collective-permute-start.1
  63.5 4.2 collective-permute-start.9
  67.7 4.2 collective-permute-start.2
  67.7 4.2 collective-permute-start.10
  71.9 4.2 collective-permute-start.3
  71.9 4.2 collective-permute-start.11
  76.1 4.2 collective-permute-start.4
  76.1 4.2 collective-permute-start.12
  80.3 4.2 collective-permute-start.5
  80.3 4.2 collective-permute-start.13
  84.5 4.2 collective-permute-start.6
  84.6 4.2 collective-permute-start.14
  88.7 4.2 collective-permute-start.7
  111.1 6.1 %copy-start.1 = (bf16[3,128,12,128]{1,3,0,2:T(8,128)(2,1)S(1)}, bf16[3,128,12,128]{1,3,0,2:T(8,128)(2,1)}, u32[]{:S(2)}) copy-start(bf16[3,128,12,128]{1,3,0,2:T(8,128)(2,1)} %get-tuple-element.311) | copy-start | bytes 3538948 | tf_op jit(solution)/shard_map/while
  115.8 1.9 copy-start
  137.4 6.1 %copy-start.1 = (bf16[3,128,12,128]{1,3,0,2:T(8,128)(2,1)S(1)}, bf16[3,128,12,128]{1,3,0,2:T(8,128)(2,1)}, u32[]{:S(2)}) copy-start(bf16[3,128,12,128]{1,3,0,2:T(8,128)(2,1)} %get-tuple-element.311) | copy-start | bytes 3538948 | tf_op jit(solution)/shard_map/while
  142.1 1.9 copy-start
  163.7 6.1 %copy-start.1 = (bf16[3,128,12,128]{1,3,0,2:T(8,128)(2,1)S(1)}, bf16[3,128,12,128]{1,3,0,2:T(8,128)(2,1)}, u32[]{:S(2)}) copy-start(bf16[3,128,12,128]{1,3,0,2:T(8,128)(2,1)} %get-tuple-element.311) | copy-start | bytes 3538948 | tf_op jit(solution)/shard_map/while
  168.4 1.9 copy-start
  190.0 6.1 %copy-start.1 = (bf16[3,128,12,128]{1,3,0,2:T(8,128)(2,1)S(1)}, bf16[3,128,12,128]{1,3,0,2:T(8,128)(2,1)}, u32[]{:S(2)}) copy-start(bf16[3,128,12,128]{1,3,0,2:T(8,128)(2,1)} %get-tuple-element.311) | copy-start | bytes 3538948 | tf_op jit(solution)/shard_map/while
  194.6 1.9 copy-start
  202.2 12.1 %all-to-all-start = ((f32[16,128,12]{1,2,0:T(8,128)}), f32[16,128,12]{1,2,0:T(8,128)S(1)}, u32[]{:S(2)}, u32[]{:S(2)}) async-start(f32[16,128,12]{1,2,0:T(8,128)} %copy.83), calls=%async_computation | async-start | bytes 262144 | tf_op jit(solution)/shard_map/all_to_all | solution.py:151
  214.3 12.3 %all-to-all-start.2 = ((f32[16,128,12]{1,2,0:T(8,128)}), f32[16,128,12]{1,2,0:T(8,128)S(1)}, u32[]{:S(2)}, u32[]{:S(2)}) async-start(f32[16,128,12]{1,2,0:T(8,128)} %copy.85), calls=%async_computation.2 | async-start | bytes 262144 | tf_op jit(solution)/shard_map/all_to_all | solution.py:152
  226.6 281.0 %all-to-all-start.1 = ((f32[16,128,1536]{1,2,0:T(8,128)}), f32[16,128,1536]{1,2,0:T(8,128)}, u32[]{:S(2)}, u32[]{:S(2)}) async-start(f32[16,128,1536]{1,2,0:T(8,128)} %bitcast_convert_fusion), calls=%async_computation.1 | async-start | bytes 25165824 | tf_op jit(solution)/shard_map/all_to_all | solution.py:150
Sparse Core Ops, SparseCore 0:
  9.5 53.7 all-gather.1
